TPU v7x, 32 devices: a whole 2x2x4 slice. The times are simulated.
32 devices in a mesh: section: 2 (over x), dp: 4 (over z), mp: 4 (over y, core).
Axes of the slice: x: 2, y: 2, z: 4, core: 2. Of those that a mesh axis runs over, the one named last changes fastest.
Arguments:
- queries: bfloat16 [2, 4, 640, 4096], P('section', 'dp', None, 'mp')
- keys: bfloat16 [2, 4, 640, 4096], P('section', 'dp', None, 'mp')
- values: bfloat16 [2, 4, 640, 4096], P('section', 'dp', None, 'mp'), may hold values from -6 to 6
- grad_out: bfloat16 [2, 4, 640, 4096], P('section', 'dp', None, 'mp'), may hold values from -6 to 6
- positions: int32 [2, 4, 640], P('section', 'dp'), may hold values from 0 to 319, as said below
Outputs:
- received: bfloat16 [2, 4, 3, 640, 4096], P('section', 'dp', None, 'mp')
- bias_grad: float32 [2, 3, 4096], P('section')
Inputs may be any that keep to these rules, and one draw needn't show every extreme that they name: `positions`: along each sequence a position is 0 or one more than the position before it; the first is 0; a document starts at token 320, and none is longer than 320 tokens.
All inputs are finite; a program needn't handle non-finite values.
Results may differ from a plain program's by a relative error of at most 0.0065.
Values may be sent and summed in bfloat16 or wider, within the bound.
No kernel may reach another device: no remote copies, remote signals or barrier semaphores. Data moves between devices by JAX's collectives and lax.ppermute only.
A program may use at most 64 MiB of HBM per device.

v0:
```python
import math
import jax
import jax.numpy as jnp
from jax import lax
from jax.sharding import PartitionSpec as P

HEAD_DIM = 128
CHUNK_HEADS = 2


def chunk_grads(query_rows, key_rows, value_rows, grad_rows, allowed, halves):
    length, width = query_rows.shape
    heads = width // HEAD_DIM
    block = length // halves
    scaling = 1.0 / math.sqrt(HEAD_DIM)

    def split(rows):
        return rows.reshape(halves, block, heads, HEAD_DIM)

    q, k, v, g = (split(query_rows), split(key_rows), split(value_rows), split(grad_rows))
    scores = jnp.einsum("bqhd,bkhd->bhqk", q, k, preferred_element_type=jnp.float32) * scaling
    scores = jnp.where(allowed[:, None], scores, jnp.float32(-1e30))
    highest = jnp.max(scores, axis=-1, keepdims=True)
    expont = jnp.exp(scores - highest)
    attn = expont / jnp.sum(expont, axis=-1, keepdims=True)
    attn_low = attn.astype(jnp.bfloat16)
    grad_v = jnp.einsum("bhqk,bqhd->bkhd", attn_low, g, preferred_element_type=jnp.float32)
    grad_attn = jnp.einsum("bqhd,bkhd->bhqk", g, v, preferred_element_type=jnp.float32)
    delta = jnp.sum(attn * grad_attn, axis=-1, keepdims=True)
    grad_scores = (attn * (grad_attn - delta) * scaling).astype(jnp.bfloat16)
    grad_q = jnp.einsum("bhqk,bkhd->bqhd", grad_scores, k, preferred_element_type=jnp.float32)
    grad_k = jnp.einsum("bhqk,bqhd->bkhd", grad_scores, q, preferred_element_type=jnp.float32)
    blocks = jnp.stack([grad_q, grad_k, grad_v]).astype(jnp.bfloat16)
    return blocks.reshape(3, length, width)


def per_device(queries, keys, values, grad_out, positions):
    query_rows = queries[0, 0]
    key_rows = keys[0, 0]
    value_rows = values[0, 0]
    grad_rows = grad_out[0, 0]
    token_positions = positions[0, 0]
    length, columns = query_rows.shape
    sections = lax.axis_size("section")
    parts = lax.axis_size("mp")
    replicas = lax.axis_size("dp")
    part = lax.axis_index("mp")
    rows = length // parts
    halves = 2
    block = length // halves
    local = jnp.arange(block, dtype=jnp.int32)
    pos = token_positions.reshape(halves, block)
    allowed = (local[None, None, :] <= local[None, :, None]) & (
        local[None, None, :] >= (local[None, :] - pos)[:, :, None]
    )

    def pairs(shift):
        return [
            ((s + 1) * parts + m, s * parts + (m + shift) % parts)
            for s in range(sections - 1)
            for m in range(parts)
        ]

    width = CHUNK_HEADS * HEAD_DIM
    chunk_count = columns // width
    arrived = [[None] * chunk_count for _ in range(parts)]
    sums = []
    for c in range(chunk_count):
        cols = slice(c * width, (c + 1) * width)
        grads = chunk_grads(
            query_rows[:, cols],
            key_rows[:, cols],
            value_rows[:, cols],
            grad_rows[:, cols],
            allowed,
            halves,
        )
        sums.append(jnp.sum(grads.astype(jnp.float32), axis=1))
        for shift in range(parts):
            target = (part + shift) % parts
            piece = lax.dynamic_slice_in_dim(grads, target * rows, rows, 1)
            arrived[shift][c] = lax.ppermute(piece, ("section", "mp"), pairs(shift))
    own = jnp.concatenate(sums, axis=1)
    slots = lax.dynamic_update_slice_in_dim(
        jnp.zeros((3, columns * parts), jnp.float32), own, part * columns, 1
    )
    totals = lax.psum(slots, ("dp", "mp"))
    totals = lax.ppermute(totals, "section", [(s + 1, s) for s in range(sections - 1)])
    bias_grad = totals / math.sqrt(replicas * length)
    received = jnp.zeros((3, rows, columns * parts), jnp.bfloat16)
    for shift in range(parts):
        source = (part - shift) % parts
        piece = jnp.concatenate(arrived[shift], axis=2)
        received = lax.dynamic_update_slice_in_dim(received, piece, source * columns, 2)
    return (received[None, None], bias_grad[None])


def solution(mesh):
    return jax.shard_map(
        per_device,
        mesh=mesh,
        in_specs=(
            P("section", "dp", None, "mp"),
            P("section", "dp", None, "mp"),
            P("section", "dp", None, "mp"),
            P("section", "dp", None, "mp"),
            P("section", "dp", None),
        ),
        out_specs=(P("section", "dp", None, "mp", None), P("section", None, None)),
        check_vma=False,
    )
```

profile of v0, /device:TPU:5, one launch (start us, length us, event | category | flops | bytes accessed | tf_op | source)
XLA Modules:
  0.0 251.5 jit_solution(15631880437137905530)
XLA Ops:
  0.7 2.3 fusion.237
  5.7 2.2 fusion.239
  10.6 1.5 fusion.135
  12.1 3.2 %fusion.256 = (f32[2,2,320]{2,1,0:T(2,128)S(1)}, f32[2,2,320,320]{2,3,1,0:T(8,128)}) fusion(pred[2,320,320]{1,2,0:T(8,128)(4,1)S(1)} %fusion.124, bf16[2,320,2,128]{3,2,1,0:T(2,128)(2,1)} %reshape.143, bf16[2,320,2,128]{3,2,1,0:T(2,128)(2,1)} %reshape.142), kind=kOutput, calls=%fused_computation.205 | convolution fusion | flops 106496320 | bytes 2503680 | tf_op jit(solution)/shard_map/sub | solution.py:24
  15.3 3.8 %fusion.75 = bf16[2,320,2,128]{3,1,2,0:T(8,128)(2,1)} fusion(f32[2,2,320,320]{2,3,1,0:T(8,128)S(1)} %fusion.135, bf16[2,320,2,128]{3,2,1,0:T(2,128)(2,1)} %reshape.143, f32[2,2,320,320]{2,3,1,0:T(8,128)} %get-tuple-element.41, f32[2,2,320]{2,1,0:T(2,128)S(1)} %get-tuple-element.40), kind=kOutput, calls=%fused_computation.57 | convolution fusion | flops 107890240 | bytes 3937280 | tf_op jit(solution)/shard_map/bhqk,bkhd->bqhd/dot_general | solution.py:31
  19.0 3.6 %fusion.72 = bf16[2,320,2,128]{3,1,2,0:T(8,128)(2,1)} fusion(f32[2,2,320,320]{2,3,1,0:T(8,128)S(1)} %fusion.135, bf16[2,320,2,128]{3,2,1,0:T(2,128)(2,1)} %reshape.142, f32[2,2,320,320]{2,3,1,0:T(8,128)} %get-tuple-element.41, f32[2,2,320]{2,1,0:T(2,128)S(1)} %get-tuple-element.40), kind=kOutput, calls=%fused_computation.56 | convolution fusion | flops 107890240 | bytes 3937280 | tf_op jit(solution)/shard_map/bhqk,bqhd->bkhd/dot_general | solution.py:32
  22.7 2.8 %fusion.96 = bf16[2,320,2,128]{3,1,2,0:T(8,128)(2,1)} fusion(bf16[2,320,2,128]{3,2,1,0:T(2,128)(2,1)} %reshape.144, f32[2,2,320,320]{2,3,1,0:T(8,128)} %get-tuple-element.41, f32[2,2,320]{2,1,0:T(2,128)S(1)} %get-tuple-element.40), kind=kOutput, calls=%fused_computation.64 | convolution fusion | flops 105840640 | bytes 2298880 | tf_op jit(solution)/shard_map/bhqk,bqhd->bkhd/dot_general | solution.py:27
  27.3 2.1 fusion.251
  29.4 1.5 fusion.133
  30.9 3.8 %fusion.81 = bf16[2,320,2,128]{3,1,2,0:T(8,128)(2,1)} fusion(f32[2,2,320,320]{2,3,1,0:T(8,128)S(1)} %fusion.133, bf16[2,320,2,128]{3,2,1,0:T(2,128)(2,1)} %copy-done.22, f32[2,2,320,320]{2,3,1,0:T(8,128)} %get-tuple-element.39, f32[2,2,320]{2,1,0:T(2,128)S(1)} %get-tuple-element.38), kind=kOutput, calls=%fused_computation.59 | convolution fusion | flops 107890240 | bytes 3937280 | tf_op jit(solution)/shard_map/bhqk,bkhd->bqhd/dot_general | solution.py:31
  34.7 3.6 %fusion.78 = bf16[2,320,2,128]{3,1,2,0:T(8,128)(2,1)} fusion(f32[2,2,320,320]{2,3,1,0:T(8,128)S(1)} %fusion.133, bf16[2,320,2,128]{3,2,1,0:T(2,128)(2,1)} %copy-done.20, f32[2,2,320,320]{2,3,1,0:T(8,128)} %get-tuple-element.39, f32[2,2,320]{2,1,0:T(2,128)S(1)} %get-tuple-element.38), kind=kOutput, calls=%fused_computation.58 | convolution fusion | flops 107890240 | bytes 3937280 | tf_op jit(solution)/shard_map/bhqk,bqhd->bkhd/dot_general | solution.py:32
  38.3 2.8 %fusion.97 = bf16[2,320,2,128]{3,1,2,0:T(8,128)(2,1)} fusion(bf16[2,320,2,128]{3,2,1,0:T(2,128)(2,1)} %reshape.148, f32[2,2,320,320]{2,3,1,0:T(8,128)} %get-tuple-element.39, f32[2,2,320]{2,1,0:T(2,128)S(1)} %get-tuple-element.38), kind=kOutput, calls=%fused_computation.65 | convolution fusion | flops 105840640 | bytes 2298880 | tf_op jit(solution)/shard_map/bhqk,bqhd->bkhd/dot_general | solution.py:27
  43.0 2.1 fusion.246
  45.1 1.5 fusion.131
  46.6 3.8 %fusion.87 = bf16[2,320,2,128]{3,1,2,0:T(8,128)(2,1)} fusion(f32[2,2,320,320]{2,3,1,0:T(8,128)S(1)} %fusion.131, bf16[2,320,2,128]{3,2,1,0:T(2,128)(2,1)} %copy-done.23, f32[2,2,320,320]{2,3,1,0:T(8,128)} %get-tuple-element.37, f32[2,2,320]{2,1,0:T(2,128)S(1)} %get-tuple-element.36), kind=kOutput, calls=%fused_computation.61 | convolution fusion | flops 107890240 | bytes 3937280 | tf_op jit(solution)/shard_map/bhqk,bkhd->bqhd/dot_general | solution.py:31
  50.4 3.6 %fusion.84 = bf16[2,320,2,128]{3,1,2,0:T(8,128)(2,1)} fusion(f32[2,2,320,320]{2,3,1,0:T(8,128)S(1)} %fusion.131, bf16[2,320,2,128]{3,2,1,0:T(2,128)(2,1)} %copy-done.21, f32[2,2,320,320]{2,3,1,0:T(8,128)} %get-tuple-element.37, f32[2,2,320]{2,1,0:T(2,128)S(1)} %get-tuple-element.36), kind=kOutput, calls=%fused_computation.60 | convolution fusion | flops 107890240 | bytes 3937280 | tf_op jit(solution)/shard_map/bhqk,bqhd->bkhd/dot_general | solution.py:32
  54.0 2.7 %fusion.98 = bf16[2,320,2,128]{3,1,2,0:T(8,128)(2,1)} fusion(bf16[2,320,2,128]{3,2,1,0:T(2,128)(2,1)} %reshape.152, f32[2,2,320,320]{2,3,1,0:T(8,128)} %get-tuple-element.37, f32[2,2,320]{2,1,0:T(2,128)S(1)} %get-tuple-element.36), kind=kOutput, calls=%fused_computation.66 | convolution fusion | flops 105840640 | bytes 2298880 | tf_op jit(solution)/shard_map/bhqk,bqhd->bkhd/dot_general | solution.py:27
  57.0 2.3 fusion.241
  59.8 3.6 %fusion.90 = bf16[2,320,2,128]{3,1,2,0:T(8,128)(2,1)} fusion(f32[2,2,320,320]{2,3,1,0:T(8,128)S(1)} %fusion.129, bf16[2,320,2,128]{3,2,1,0:T(2,128)(2,1)S(1)} %reshape.154, f32[2,2,320,320]{2,3,1,0:T(8,128)} %get-tuple-element.35, f32[2,2,320]{2,1,0:T(2,128)S(1)} %get-tuple-element.34), kind=kOutput, calls=%fused_computation.62 | convolution fusion | flops 107890240 | bytes 3937280 | tf_op jit(solution)/shard_map/bhqk,bqhd->bkhd/dot_general | solution.py:32
  63.4 3.7 %fusion.93 = bf16[2,320,2,128]{3,1,2,0:T(8,128)(2,1)} fusion(f32[2,2,320,320]{2,3,1,0:T(8,128)S(1)} %fusion.129, bf16[2,320,2,128]{3,2,1,0:T(2,128)(2,1)S(1)} %reshape.155, f32[2,2,320,320]{2,3,1,0:T(8,128)} %get-tuple-element.35, f32[2,2,320]{2,1,0:T(2,128)S(1)} %get-tuple-element.34), kind=kOutput, calls=%fused_computation.63 | convolution fusion | flops 107890240 | bytes 3937280 | tf_op jit(solution)/shard_map/bhqk,bkhd->bqhd/dot_general | solution.py:31
  67.1 2.7 %fusion.99 = bf16[2,320,2,128]{3,1,2,0:T(8,128)(2,1)} fusion(bf16[2,320,2,128]{3,2,1,0:T(2,128)(2,1)S(1)} %reshape.156, f32[2,2,320,320]{2,3,1,0:T(8,128)} %get-tuple-element.35, f32[2,2,320]{2,1,0:T(2,128)S(1)} %get-tuple-element.34), kind=kOutput, calls=%fused_computation.67 | convolution fusion | flops 105840640 | bytes 2298880 | tf_op jit(solution)/shard_map/bhqk,bqhd->bkhd/dot_general | solution.py:27
  75.5 2.0 copy.41
  78.7 2.0 copy.43
  80.7 1.9 stack.58
  86.1 2.0 copy.50
  88.2 1.9 stack.60
  90.1 1.7 constant_dynamic-update-slice_fusion.11
  91.8 2.0 copy.54
  93.8 1.9 stack.62
  96.4 1.7 constant_dynamic-update-slice_fusion.9
  99.6 53.4 %psum.7 = f32[3,4096]{1,0:T(4,128)} all-reduce(f32[3,4096]{1,0:T(4,128)S(1)} %maximum_dynamic-update-slice_fusion), channel_id=1, replica_groups=mesh['section'=2,'dp'=4,'mp'=4] {'dp','mp'}, use_global_device_ids=true, to_apply=%region_16.17 | all-reduce | flops 12288 | bytes 98304 | tf_op jit(solution)/shard_map/psum | solution.py:87
  155.1 1.4 collective-permute-start
  157.4 1.4 collective-permute-start.1
  165.9 1.5 collective-permute-done.1
  168.7 4.0 %collective-permute-done.2 = bf16[3,160,256]{2,1,0:T(8,128)(2,1)S(1)} collective-permute-done((bf16[3,160,256]{2,1,0:T(8,128)(2,1)}, bf16[3,160,256]{2,1,0:T(8,128)(2,1)S(1)}, u32[]{:S(2)}, u32[]{:S(2)}) %collective-permute-start.2) | collective-permute-done | bytes 245792 | tf_op jit(solution)/shard_map/ppermute | solution.py:82
  174.0 3.9 %collective-permute-done.3 = bf16[3,160,256]{2,1,0:T(8,128)(2,1)S(1)} collective-permute-done((bf16[3,160,256]{2,1,0:T(8,128)(2,1)}, bf16[3,160,256]{2,1,0:T(8,128)(2,1)S(1)}, u32[]{:S(2)}, u32[]{:S(2)}) %collective-permute-start.3) | collective-permute-done | bytes 245792 | tf_op jit(solution)/shard_map/ppermute | solution.py:82
  179.1 12.5 %collective-permute-done.4 = bf16[3,160,256]{2,1,0:T(8,128)(2,1)S(1)} collective-permute-done((bf16[3,160,256]{2,1,0:T(8,128)(2,1)}, bf16[3,160,256]{2,1,0:T(8,128)(2,1)S(1)}, u32[]{:S(2)}, u32[]{:S(2)}) %collective-permute-start.4) | collective-permute-done | bytes 245792 | tf_op jit(solution)/shard_map/ppermute | solution.py:82
  193.0 4.0 %collective-permute-done.5 = bf16[3,160,256]{2,1,0:T(8,128)(2,1)S(1)} collective-permute-done((bf16[3,160,256]{2,1,0:T(8,128)(2,1)}, bf16[3,160,256]{2,1,0:T(8,128)(2,1)S(1)}, u32[]{:S(2)}, u32[]{:S(2)}) %collective-permute-start.5) | collective-permute-done | bytes 245792 | tf_op jit(solution)/shard_map/ppermute | solution.py:82
  198.9 3.3 %collective-permute-done.6 = bf16[3,160,256]{2,1,0:T(8,128)(2,1)S(1)} collective-permute-done((bf16[3,160,256]{2,1,0:T(8,128)(2,1)S(1)}, bf16[3,160,256]{2,1,0:T(8,128)(2,1)S(1)}, u32[]{:S(2)}, u32[]{:S(2)}) %collective-permute-start.6) | collective-permute-done | bytes 245792 | tf_op jit(solution)/shard_map/ppermute | solution.py:82
  205.1 2.0 collective-permute-done.7
  209.8 4.1 %collective-permute-done.9 = bf16[3,160,256]{2,1,0:T(8,128)(2,1)S(1)} collective-permute-done((bf16[3,160,256]{2,1,0:T(8,128)(2,1)S(1)}, bf16[3,160,256]{2,1,0:T(8,128)(2,1)S(1)}, u32[]{:S(2)}, u32[]{:S(2)}) %collective-permute-start.9) | collective-permute-done | bytes 245792 | tf_op jit(solution)/shard_map/ppermute | solution.py:82
  215.1 4.0 %collective-permute-done.10 = bf16[3,160,256]{2,1,0:T(8,128)(2,1)S(1)} collective-permute-done((bf16[3,160,256]{2,1,0:T(8,128)(2,1)S(1)}, bf16[3,160,256]{2,1,0:T(8,128)(2,1)S(1)}, u32[]{:S(2)}, u32[]{:S(2)}) %collective-permute-start.10) | collective-permute-done | bytes 245792 | tf_op jit(solution)/shard_map/ppermute | solution.py:82
  220.5 3.9 %collective-permute-done.11 = bf16[3,160,256]{2,1,0:T(8,128)(2,1)S(1)} collective-permute-done((bf16[3,160,256]{2,1,0:T(8,128)(2,1)S(1)}, bf16[3,160,256]{2,1,0:T(8,128)(2,1)S(1)}, u32[]{:S(2)}, u32[]{:S(2)}) %collective-permute-start.11) | collective-permute-done | bytes 245792 | tf_op jit(solution)/shard_map/ppermute | solution.py:82
  224.5 13.4 %collective-permute-done.12 = bf16[3,160,256]{2,1,0:T(8,128)(2,1)S(1)} collective-permute-done((bf16[3,160,256]{2,1,0:T(8,128)(2,1)S(1)}, bf16[3,160,256]{2,1,0:T(8,128)(2,1)S(1)}, u32[]{:S(2)}, u32[]{:S(2)}) %collective-permute-start.12) | collective-permute-done | bytes 245792 | tf_op jit(solution)/shard_map/ppermute | solution.py:82
  237.9 5.3 %collective-permute-done.13 = bf16[3,160,256]{2,1,0:T(8,128)(2,1)S(1)} collective-permute-done((bf16[3,160,256]{2,1,0:T(8,128)(2,1)S(1)}, bf16[3,160,256]{2,1,0:T(8,128)(2,1)S(1)}, u32[]{:S(2)}, u32[]{:S(2)}) %collective-permute-start.13) | collective-permute-done | bytes 245792 | tf_op jit(solution)/shard_map/ppermute | solution.py:82
  243.2 3.6 %collective-permute-done.14 = bf16[3,160,256]{2,1,0:T(8,128)(2,1)S(1)} collective-permute-done((bf16[3,160,256]{2,1,0:T(8,128)(2,1)S(1)}, bf16[3,160,256]{2,1,0:T(8,128)(2,1)S(1)}, u32[]{:S(2)}, u32[]{:S(2)}) %collective-permute-start.14) | collective-permute-done | bytes 245792 | tf_op jit(solution)/shard_map/ppermute | solution.py:82
  246.8 2.6 %collective-permute-done.15 = bf16[3,160,256]{2,1,0:T(8,128)(2,1)S(1)} collective-permute-done((bf16[3,160,256]{2,1,0:T(8,128)(2,1)S(1)}, bf16[3,160,256]{2,1,0:T(8,128)(2,1)S(1)}, u32[]{:S(2)}, u32[]{:S(2)}) %collective-permute-start.15) | collective-permute-done | bytes 245792 | tf_op jit(solution)/shard_map/ppermute | solution.py:82
  249.6 1.9 copy-done.1
  (139 shorter events, 47.4 us)
Async XLA Ops:
  0.6 3.2 %copy-start.10 = (bf16[1,1,640,1024]{3,2,1,0:T(8,128)(2,1)S(1)}, bf16[1,1,640,1024]{3,2,1,0:T(8,128)(2,1)}, u32[]{:S(2)}) copy-start(bf16[1,1,640,1024]{3,2,1,0:T(8,128)(2,1)} %param.6) | copy-start | bytes 3932164
  3.0 2.5 %copy-start.26 = (s32[1,1,640]{2,1,0:T(1,128)S(1)}, s32[1,1,640]{2,1,0:T(1,128)}, u32[]{:S(2)}) copy-start(s32[1,1,640]{2,1,0:T(1,128)} %param.9) | copy-start | bytes 7684
  4.8 3.9 %copy-start.11 = (bf16[1,1,640,1024]{3,2,1,0:T(8,128)(2,1)S(1)}, bf16[1,1,640,1024]{3,2,1,0:T(8,128)(2,1)}, u32[]{:S(2)}) copy-start(bf16[1,1,640,1024]{3,2,1,0:T(8,128)(2,1)} %param.7) | copy-start | bytes 3932164
  22.7 2.8 %copy-start.6 = (bf16[640,256]{1,0:T(8,128)(2,1)S(1)}, bf16[640,256]{1,0:T(8,128)(2,1)}, u32[]{:S(2)}) copy-start(bf16[640,256]{1,0:T(8,128)(2,1)} %get-tuple-element.5) | copy-start | bytes 983044
  22.7 2.9 %copy-start.7 = (bf16[640,256]{1,0:T(8,128)(2,1)S(1)}, bf16[640,256]{1,0:T(8,128)(2,1)}, u32[]{:S(2)}) copy-start(bf16[640,256]{1,0:T(8,128)(2,1)} %get-tuple-element.9) | copy-start | bytes 983044
  22.7 3.0 %copy-start.8 = (bf16[640,256]{1,0:T(8,128)(2,1)S(1)}, bf16[640,256]{1,0:T(8,128)(2,1)}, u32[]{:S(2)}) copy-start(bf16[640,256]{1,0:T(8,128)(2,1)} %get-tuple-element.13) | copy-start | bytes 983044
  25.5 1.0 copy-start.9
  25.5 1.7 copy-start.20
  25.7 1.6 copy-start.22
  38.3 2.8 %copy-start.2 = (bf16[640,256]{1,0:T(8,128)(2,1)S(1)}, bf16[640,256]{1,0:T(8,128)(2,1)}, u32[]{:S(2)}) copy-start(bf16[640,256]{1,0:T(8,128)(2,1)} %get-tuple-element.4) | copy-start | bytes 983044
  38.3 2.9 %copy-start.3 = (bf16[640,256]{1,0:T(8,128)(2,1)S(1)}, bf16[640,256]{1,0:T(8,128)(2,1)}, u32[]{:S(2)}) copy-start(bf16[640,256]{1,0:T(8,128)(2,1)} %get-tuple-element.8) | copy-start | bytes 983044
  38.3 3.0 %copy-start.4 = (bf16[640,256]{1,0:T(8,128)(2,1)S(1)}, bf16[640,256]{1,0:T(8,128)(2,1)}, u32[]{:S(2)}) copy-start(bf16[640,256]{1,0:T(8,128)(2,1)} %get-tuple-element.12) | copy-start | bytes 983044
  41.1 1.0 copy-start.5
  41.2 1.8 copy-start.21
  41.3 1.7 copy-start.23
  67.1 2.7 %copy-start.16 = (bf16[2,320,2,128]{3,1,2,0:T(8,128)(2,1)S(1)}, bf16[2,320,2,128]{3,1,2,0:T(8,128)(2,1)}, u32[]{:S(2)}) copy-start(bf16[2,320,2,128]{3,1,2,0:T(8,128)(2,1)} %fusion.75) | copy-start | bytes 983044
  69.8 1.0 copy-start.13
  69.8 1.5 copy-start.12
  71.4 1.0 copy-start.17
  72.0 1.0 copy-start.15
  72.0 1.5 copy-start.14
  73.9 1.0 copy-start.18
  82.6 1.2 copy-start.19
  152.9 10.2 %collective-permute-start.16 = (f32[3,4096]{1,0:T(4,128)}, f32[3,4096]{1,0:T(4,128)S(1)}, u32[]{:S(2)}, u32[]{:S(2)}) collective-permute-start(f32[3,4096]{1,0:T(4,128)} %psum.7), channel_id=1, source_target_pairs={{16,0},{17,1},{18,2},{19,3},{20,4},{21,5},{22,6},{23,7},{24,8},{25... | collective-permute-start | bytes 147464 | tf_op jit(solution)/shard_map/ppermute | solution.py:88
  155.1 6.0 %copy-start = (bf16[3,640,256]{2,1,0:T(8,128)(2,1)S(1)}, bf16[3,640,256]{2,1,0:T(8,128)(2,1)}, u32[]{:S(2)}) copy-start(bf16[3,640,256]{2,1,0:T(8,128)(2,1)} %constant_dynamic-update-slice_fusion.9) | copy-start | bytes 2949124
  155.1 9.4 %collective-permute-start = (bf16[3,160,256]{2,1,0:T(8,128)(2,1)S(1)}, bf16[3,160,256]{2,1,0:T(8,128)(2,1)}, u32[]{:S(2)}, u32[]{:S(2)}) collective-permute-start(bf16[3,160,256]{2,1,0:T(8,128)(2,1)S(1)} %get-tuple-element.21), channel_id=1, source_target_pairs={{16,0},{17,1},{18,2},{19,3},{20,4},{21,5},{22,6},{23,7},{24,8},{25... | collective-permute-start | bytes 737288 | tf_op jit(solution)/shard_map/ppermute | solution.py:82
  157.4 34.3 %copy-start.24 = (bf16[3,160,256]{2,1,0:T(8,128)(2,1)S(1)}, bf16[3,160,256]{2,1,0:T(8,128)(2,1)}, u32[]{:S(2)}) copy-start(bf16[3,160,256]{2,1,0:T(8,128)(2,1)} %get-tuple-element.23) | copy-start | bytes 737284
  157.4 10.0 %collective-permute-start.1 = (bf16[3,160,256]{2,1,0:T(8,128)(2,1)}, bf16[3,160,256]{2,1,0:T(8,128)(2,1)}, u32[]{:S(2)}, u32[]{:S(2)}) collective-permute-start(bf16[3,160,256]{2,1,0:T(8,128)(2,1)} %get-tuple-element.25), channel_id=1, source_target_pairs={{16,0},{17,1},{18,2},{19,3},{20,4},{21,5},{22,6},{23,7},{24,8},{25... | collective-permute-start | bytes 737288 | tf_op jit(solution)/shard_map/ppermute | solution.py:82
  159.7 7.7 %copy-start.25 = (bf16[3,160,256]{2,1,0:T(8,128)(2,1)S(1)}, bf16[3,160,256]{2,1,0:T(8,128)(2,1)}, u32[]{:S(2)}) copy-start(bf16[3,160,256]{2,1,0:T(8,128)(2,1)} %get-tuple-element.28) | copy-start | bytes 737284
  159.7 13.0 %collective-permute-start.2 = (bf16[3,160,256]{2,1,0:T(8,128)(2,1)}, bf16[3,160,256]{2,1,0:T(8,128)(2,1)S(1)}, u32[]{:S(2)}, u32[]{:S(2)}) collective-permute-start(bf16[3,160,256]{2,1,0:T(8,128)(2,1)} %get-tuple-element.29), channel_id=1, source_target_pairs={{16,0},{17,1},{18,2},{19,3},{20,4},{21,5},{22,6},{23,7},{24,8},{25... | collective-permute-start | bytes 737288 | tf_op jit(solution)/shard_map/ppermute | solution.py:82
  161.9 16.0 %collective-permute-start.3 = (bf16[3,160,256]{2,1,0:T(8,128)(2,1)}, bf16[3,160,256]{2,1,0:T(8,128)(2,1)S(1)}, u32[]{:S(2)}, u32[]{:S(2)}) collective-permute-start(bf16[3,160,256]{2,1,0:T(8,128)(2,1)} %get-tuple-element.33), channel_id=1, source_target_pairs={{16,0},{17,1},{18,2},{19,3},{20,4},{21,5},{22,6},{23,7},{24,8},{25... | collective-permute-start | bytes 737288 | tf_op jit(solution)/shard_map/ppermute | solution.py:82
  163.2 28.5 %collective-permute-start.4 = (bf16[3,160,256]{2,1,0:T(8,128)(2,1)}, bf16[3,160,256]{2,1,0:T(8,128)(2,1)S(1)}, u32[]{:S(2)}, u32[]{:S(2)}) collective-permute-start(bf16[3,160,256]{2,1,0:T(8,128)(2,1)} %get-tuple-element.20), channel_id=1, source_target_pairs={{16,1},{17,2},{18,3},{19,0},{20,5},{21,6},{22,7},{23,4},{24,9},{25... | collective-permute-start | bytes 737288 | tf_op jit(solution)/shard_map/ppermute | solution.py:82
  164.5 32.4 %collective-permute-start.5 = (bf16[3,160,256]{2,1,0:T(8,128)(2,1)}, bf16[3,160,256]{2,1,0:T(8,128)(2,1)S(1)}, u32[]{:S(2)}, u32[]{:S(2)}) collective-permute-start(bf16[3,160,256]{2,1,0:T(8,128)(2,1)} %get-tuple-element.24), channel_id=1, source_target_pairs={{16,1},{17,2},{18,3},{19,0},{20,5},{21,6},{22,7},{23,4},{24,9},{25... | collective-permute-start | bytes 737288 | tf_op jit(solution)/shard_map/ppermute | solution.py:82
  167.4 34.8 %collective-permute-start.6 = (bf16[3,160,256]{2,1,0:T(8,128)(2,1)S(1)}, bf16[3,160,256]{2,1,0:T(8,128)(2,1)S(1)}, u32[]{:S(2)}, u32[]{:S(2)}) collective-permute-start(bf16[3,160,256]{2,1,0:T(8,128)(2,1)S(1)} %copy-done.25), channel_id=1, source_target_pairs={{16,1},{17,2},{18,3},{19,0},{20,5},{21,6},{22,7},{23,4},{24,9},{25... | collective-permute-start | bytes 737288 | tf_op jit(solution)/shard_map/ppermute | solution.py:82
  172.7 34.5 %collective-permute-start.7 = (bf16[3,160,256]{2,1,0:T(8,128)(2,1)S(1)}, bf16[3,160,256]{2,1,0:T(8,128)(2,1)S(1)}, u32[]{:S(2)}, u32[]{:S(2)}) collective-permute-start(bf16[3,160,256]{2,1,0:T(8,128)(2,1)S(1)} %get-tuple-element.32), channel_id=1, source_target_pairs={{16,1},{17,2},{18,3},{19,0},{20,5},{21,6},{22,7},{23,4},{24,9},{25... | collective-permute-start | bytes 737288 | tf_op jit(solution)/shard_map/ppermute | solution.py:82
  177.8 30.6 %collective-permute-start.8 = (bf16[3,160,256]{2,1,0:T(8,128)(2,1)S(1)}, bf16[3,160,256]{2,1,0:T(8,128)(2,1)S(1)}, u32[]{:S(2)}, u32[]{:S(2)}) collective-permute-start(bf16[3,160,256]{2,1,0:T(8,128)(2,1)S(1)} %get-tuple-element.19), channel_id=1, source_target_pairs={{16,2},{17,3},{18,0},{19,1},{20,6},{21,7},{22,4},{23,5},{24,10},{2... | collective-permute-start | bytes 737288 | tf_op jit(solution)/shard_map/ppermute | solution.py:82
  191.7 22.2 %collective-permute-start.9 = (bf16[3,160,256]{2,1,0:T(8,128)(2,1)S(1)}, bf16[3,160,256]{2,1,0:T(8,128)(2,1)S(1)}, u32[]{:S(2)}, u32[]{:S(2)}) collective-permute-start(bf16[3,160,256]{2,1,0:T(8,128)(2,1)S(1)} %copy-done.24), channel_id=1, source_target_pairs={{16,2},{17,3},{18,0},{19,1},{20,6},{21,7},{22,4},{23,5},{24,10},{2... | collective-permute-start | bytes 737288 | tf_op jit(solution)/shard_map/ppermute | solution.py:82
  196.9 22.2 %collective-permute-start.10 = (bf16[3,160,256]{2,1,0:T(8,128)(2,1)S(1)}, bf16[3,160,256]{2,1,0:T(8,128)(2,1)S(1)}, u32[]{:S(2)}, u32[]{:S(2)}) collective-permute-start(bf16[3,160,256]{2,1,0:T(8,128)(2,1)S(1)} %get-tuple-element.27), channel_id=1, source_target_pairs={{16,2},{17,3},{18,0},{19,1},{20,6},{21,7},{22,4},{23,5},{24,10},{2... | collective-permute-start | bytes 737288 | tf_op jit(solution)/shard_map/ppermute | solution.py:82
  202.2 22.2 %collective-permute-start.11 = (bf16[3,160,256]{2,1,0:T(8,128)(2,1)S(1)}, bf16[3,160,256]{2,1,0:T(8,128)(2,1)S(1)}, u32[]{:S(2)}, u32[]{:S(2)}) collective-permute-start(bf16[3,160,256]{2,1,0:T(8,128)(2,1)S(1)} %get-tuple-element.31), channel_id=1, source_target_pairs={{16,2},{17,3},{18,0},{19,1},{20,6},{21,7},{22,4},{23,5},{24,10},{2... | collective-permute-start | bytes 737288 | tf_op jit(solution)/shard_map/ppermute | solution.py:82
  207.2 30.7 %collective-permute-start.12 = (bf16[3,160,256]{2,1,0:T(8,128)(2,1)S(1)}, bf16[3,160,256]{2,1,0:T(8,128)(2,1)S(1)}, u32[]{:S(2)}, u32[]{:S(2)}) collective-permute-start(bf16[3,160,256]{2,1,0:T(8,128)(2,1)S(1)} %get-tuple-element.18), channel_id=1, source_target_pairs={{16,3},{17,0},{18,1},{19,2},{20,7},{21,4},{22,5},{23,6},{24,11},{2... | collective-permute-start | bytes 737288 | tf_op jit(solution)/shard_map/ppermute | solution.py:82
  208.5 34.7 %collective-permute-start.13 = (bf16[3,160,256]{2,1,0:T(8,128)(2,1)S(1)}, bf16[3,160,256]{2,1,0:T(8,128)(2,1)S(1)}, u32[]{:S(2)}, u32[]{:S(2)}) collective-permute-start(bf16[3,160,256]{2,1,0:T(8,128)(2,1)S(1)} %get-tuple-element.22), channel_id=1, source_target_pairs={{16,3},{17,0},{18,1},{19,2},{20,7},{21,4},{22,5},{23,6},{24,11},{2... | collective-permute-start | bytes 737288 | tf_op jit(solution)/shard_map/ppermute | solution.py:82
  213.8 33.0 %collective-permute-start.14 = (bf16[3,160,256]{2,1,0:T(8,128)(2,1)S(1)}, bf16[3,160,256]{2,1,0:T(8,128)(2,1)S(1)}, u32[]{:S(2)}, u32[]{:S(2)}) collective-permute-start(bf16[3,160,256]{2,1,0:T(8,128)(2,1)S(1)} %get-tuple-element.26), channel_id=1, source_target_pairs={{16,3},{17,0},{18,1},{19,2},{20,7},{21,4},{22,5},{23,6},{24,11},{2... | collective-permute-start | bytes 737288 | tf_op jit(solution)/shard_map/ppermute | solution.py:82
  219.1 30.3 %collective-permute-start.15 = (bf16[3,160,256]{2,1,0:T(8,128)(2,1)S(1)}, bf16[3,160,256]{2,1,0:T(8,128)(2,1)S(1)}, u32[]{:S(2)}, u32[]{:S(2)}) collective-permute-start(bf16[3,160,256]{2,1,0:T(8,128)(2,1)S(1)} %get-tuple-element.30), channel_id=1, source_target_pairs={{16,3},{17,0},{18,1},{19,2},{20,7},{21,4},{22,5},{23,6},{24,11},{2... | collective-permute-start | bytes 737288 | tf_op jit(solution)/shard_map/ppermute | solution.py:82
  249.5 1.9 copy-start.1
where the time goes:
time: 253 us; the launch traced here: 251 us
  waiting for transfers between devices  68.1 us (27%)
  matrix products  55.1 us (22%)
  blocking collectives  53.4 us (21%)
  local copies, waits for them, and re-layouts  47.7 us (19%)
  starting transfers between devices  22.2 us (9%)
  other arithmetic  3.64 us (1%)
    ppermute x16, waiting for transfers between devices, per_device(): arrived[shift][c] = lax.ppermute(piece, ('section', 'mp'), pairs(shift))  68.1 us
    psum x1, blocking collectives, per_device(): totals = lax.psum(slots, ('dp', 'mp'))  53.4 us
    ppermute x16, starting transfers between devices, per_device(): arrived[shift][c] = lax.ppermute(piece, ('section', 'mp'), pairs(shift))  20.9 us
    dot_general x4, matrix products, chunk_grads(): jnp.einsum('bhqk,bkhd->bqhd', grad_scores, k, preferred_element_type=jnp....  15.1 us
    dot_general x4, matrix products, chunk_grads(): jnp.einsum('bhqk,bqhd->bkhd', grad_scores, q, preferred_element_type=jnp....  14.5 us
    another operation x16, local copies, waits for them, and re-layouts, chunk_grads(): blocks = jnp.stack([grad_q, grad_k, grad_v]).astype(jnp.bfloat16)  12.4 us
    dot_general x4, matrix products, chunk_grads(): jnp.einsum('bhqk,bqhd->bkhd', attn_low, g, preferred_element_type=jnp.flo...  11 us
    sub x4, matrix products, chunk_grads(): expont = jnp.exp(scores - highest)  9.71 us
  transfers between devices with their start and end apart: 17, of which 14 were waited for; matrix products, arithmetic and copies ran while one was open for 2% of the time, Pallas kernels for 0%

commit v1 on v0

--- a/solution.py
+++ b/solution.py
@@ -84,7 +84,8 @@
     slots = lax.dynamic_update_slice_in_dim(
         jnp.zeros((3, columns * parts), jnp.float32), own, part * columns, 1
     )
-    totals = lax.psum(slots, ("dp", "mp"))
+    half = lax.psum(slots, "mp")
+    totals = lax.psum(half, "dp")
     totals = lax.ppermute(totals, "section", [(s + 1, s) for s in range(sections - 1)])
     bias_grad = totals / math.sqrt(replicas * length)
     received = jnp.zeros((3, rows, columns * parts), jnp.bfloat16)

time: 253 us -> 224 us (0.89)
  blocking collectives: 53.4 us -> 27.9 us
  waiting for transfers between devices: 68.1 us -> 63.4 us
    psum x1 -> x2, blocking collectives: 53.4 us -> 27.9 us  [the longest x1 16.8 us: per_device(): totals = lax.psum(half, 'dp')]
    ppermute x16, waiting for transfers between devices: 68.1 us -> 63.4 us  [per_device(): arrived[shift][c] = lax.ppermute(piece, ('section', 'mp'), pairs(shift))]
  transfers between devices with their start and end apart: 17 -> 17, of which waited for: 14 -> 13; matrix products, arithmetic and copies ran while one was open for 2% -> 3% of each run, Pallas kernels for 0% -> 0%
where the time goes in v1:
time: 224 us; the launch traced here: 221 us
  waiting for transfers between devices  63.4 us (28%)
  matrix products  55.1 us (25%)
  local copies, waits for them, and re-layouts  47.7 us (21%)
  blocking collectives  27.9 us (12%)
  starting transfers between devices  22.2 us (10%)
  other arithmetic  3.64 us (2%)
    ppermute x16, waiting for transfers between devices, per_device(): arrived[shift][c] = lax.ppermute(piece, ('section', 'mp'), pairs(shift))  63.4 us
    ppermute x16, starting transfers between devices, per_device(): arrived[shift][c] = lax.ppermute(piece, ('section', 'mp'), pairs(shift))  20.9 us
    psum x1, blocking collectives, per_device(): totals = lax.psum(half, 'dp')  16.8 us
    dot_general x4, matrix products, chunk_grads(): jnp.einsum('bhqk,bkhd->bqhd', grad_scores, k, preferred_element_type=jnp....  15.1 us
    dot_general x4, matrix products, chunk_grads(): jnp.einsum('bhqk,bqhd->bkhd', grad_scores, q, preferred_element_type=jnp....  14.5 us
    another operation x16, local copies, waits for them, and re-layouts, chunk_grads(): blocks = jnp.stack([grad_q, grad_k, grad_v]).astype(jnp.bfloat16)  12.4 us
    psum x1, blocking collectives, per_device(): half = lax.psum(slots, 'mp')  11 us
    dot_general x4, matrix products, chunk_grads(): jnp.einsum('bhqk,bqhd->bkhd', attn_low, g, preferred_element_type=jnp.flo...  11 us
  transfers between devices with their start and end apart: 17, of which 13 were waited for; matrix products, arithmetic and copies ran while one was open for 3% of the time, Pallas kernels for 0%

profile of v1, /device:TPU:5, one launch (start us, length us, event | category | flops | bytes accessed | tf_op | source)
XLA Modules:
  0.0 221.3 jit_solution(6763914935326599817)
XLA Ops:
  0.7 2.3 %fusion.237 = (bf16[640,256]{1,0:T(8,128)(2,1)S(1)}, bf16[640,256]{1,0:T(8,128)(2,1)S(1)}, bf16[640,256]{1,0:T(8,128)(2,1)}, bf16[640,256]{1,0:T(8,128)(2,1)}) fusion(bf16[640,1024]{1,0:T(8,128)(2,1)} %bitcast.44), kind=kLoop, calls=%fused_computation.198 | loop fusion | bytes 2621440 | tf_op jit(solution)/shard_map/slice | solution.py:71
  5.7 2.2 %fusion.239 = (bf16[640,256]{1,0:T(8,128)(2,1)S(1)}, bf16[640,256]{1,0:T(8,128)(2,1)S(1)}, bf16[640,256]{1,0:T(8,128)(2,1)}, bf16[640,256]{1,0:T(8,128)(2,1)}) fusion(bf16[640,1024]{1,0:T(8,128)(2,1)} %bitcast.46), kind=kLoop, calls=%fused_computation.200 | loop fusion | bytes 2621440 | tf_op jit(solution)/shard_map/slice | solution.py:74
  10.6 1.5 fusion.135
  12.1 3.2 %fusion.256 = (f32[2,2,320]{2,1,0:T(2,128)S(1)}, f32[2,2,320,320]{2,3,1,0:T(8,128)}) fusion(pred[2,320,320]{1,2,0:T(8,128)(4,1)S(1)} %fusion.124, bf16[2,320,2,128]{3,2,1,0:T(2,128)(2,1)} %reshape.143, bf16[2,320,2,128]{3,2,1,0:T(2,128)(2,1)} %reshape.142), kind=kOutput, calls=%fused_computation.205 | convolution fusion | flops 106496320 | bytes 2503680 | tf_op jit(solution)/shard_map/sub | solution.py:24
  15.3 3.8 %fusion.75 = bf16[2,320,2,128]{3,1,2,0:T(8,128)(2,1)} fusion(f32[2,2,320,320]{2,3,1,0:T(8,128)S(1)} %fusion.135, bf16[2,320,2,128]{3,2,1,0:T(2,128)(2,1)} %reshape.143, f32[2,2,320,320]{2,3,1,0:T(8,128)} %get-tuple-element.41, f32[2,2,320]{2,1,0:T(2,128)S(1)} %get-tuple-element.40), kind=kOutput, calls=%fused_computation.57 | convolution fusion | flops 107890240 | bytes 3937280 | tf_op jit(solution)/shard_map/bhqk,bkhd->bqhd/dot_general | solution.py:31
  19.0 3.6 %fusion.72 = bf16[2,320,2,128]{3,1,2,0:T(8,128)(2,1)} fusion(f32[2,2,320,320]{2,3,1,0:T(8,128)S(1)} %fusion.135, bf16[2,320,2,128]{3,2,1,0:T(2,128)(2,1)} %reshape.142, f32[2,2,320,320]{2,3,1,0:T(8,128)} %get-tuple-element.41, f32[2,2,320]{2,1,0:T(2,128)S(1)} %get-tuple-element.40), kind=kOutput, calls=%fused_computation.56 | convolution fusion | flops 107890240 | bytes 3937280 | tf_op jit(solution)/shard_map/bhqk,bqhd->bkhd/dot_general | solution.py:32
  22.7 2.8 %fusion.96 = bf16[2,320,2,128]{3,1,2,0:T(8,128)(2,1)} fusion(bf16[2,320,2,128]{3,2,1,0:T(2,128)(2,1)} %reshape.144, f32[2,2,320,320]{2,3,1,0:T(8,128)} %get-tuple-element.41, f32[2,2,320]{2,1,0:T(2,128)S(1)} %get-tuple-element.40), kind=kOutput, calls=%fused_computation.64 | convolution fusion | flops 105840640 | bytes 2298880 | tf_op jit(solution)/shard_map/bhqk,bqhd->bkhd/dot_general | solution.py:27
  27.3 2.1 fusion.251
  29.4 1.5 fusion.133
  30.9 3.8 %fusion.81 = bf16[2,320,2,128]{3,1,2,0:T(8,128)(2,1)} fusion(f32[2,2,320,320]{2,3,1,0:T(8,128)S(1)} %fusion.133, bf16[2,320,2,128]{3,2,1,0:T(2,128)(2,1)} %copy-done.22, f32[2,2,320,320]{2,3,1,0:T(8,128)} %get-tuple-element.39, f32[2,2,320]{2,1,0:T(2,128)S(1)} %get-tuple-element.38), kind=kOutput, calls=%fused_computation.59 | convolution fusion | flops 107890240 | bytes 3937280 | tf_op jit(solution)/shard_map/bhqk,bkhd->bqhd/dot_general | solution.py:31
  34.7 3.6 %fusion.78 = bf16[2,320,2,128]{3,1,2,0:T(8,128)(2,1)} fusion(f32[2,2,320,320]{2,3,1,0:T(8,128)S(1)} %fusion.133, bf16[2,320,2,128]{3,2,1,0:T(2,128)(2,1)} %copy-done.20, f32[2,2,320,320]{2,3,1,0:T(8,128)} %get-tuple-element.39, f32[2,2,320]{2,1,0:T(2,128)S(1)} %get-tuple-element.38), kind=kOutput, calls=%fused_computation.58 | convolution fusion | flops 107890240 | bytes 3937280 | tf_op jit(solution)/shard_map/bhqk,bqhd->bkhd/dot_general | solution.py:32
  38.3 2.8 %fusion.97 = bf16[2,320,2,128]{3,1,2,0:T(8,128)(2,1)} fusion(bf16[2,320,2,128]{3,2,1,0:T(2,128)(2,1)} %reshape.148, f32[2,2,320,320]{2,3,1,0:T(8,128)} %get-tuple-element.39, f32[2,2,320]{2,1,0:T(2,128)S(1)} %get-tuple-element.38), kind=kOutput, calls=%fused_computation.65 | convolution fusion | flops 105840640 | bytes 2298880 | tf_op jit(solution)/shard_map/bhqk,bqhd->bkhd/dot_general | solution.py:27
  43.0 2.1 fusion.246
  45.1 1.5 fusion.131
  46.6 3.8 %fusion.87 = bf16[2,320,2,128]{3,1,2,0:T(8,128)(2,1)} fusion(f32[2,2,320,320]{2,3,1,0:T(8,128)S(1)} %fusion.131, bf16[2,320,2,128]{3,2,1,0:T(2,128)(2,1)} %copy-done.23, f32[2,2,320,320]{2,3,1,0:T(8,128)} %get-tuple-element.37, f32[2,2,320]{2,1,0:T(2,128)S(1)} %get-tuple-element.36), kind=kOutput, calls=%fused_computation.61 | convolution fusion | flops 107890240 | bytes 3937280 | tf_op jit(solution)/shard_map/bhqk,bkhd->bqhd/dot_general | solution.py:31
  50.4 3.6 %fusion.84 = bf16[2,320,2,128]{3,1,2,0:T(8,128)(2,1)} fusion(f32[2,2,320,320]{2,3,1,0:T(8,128)S(1)} %fusion.131, bf16[2,320,2,128]{3,2,1,0:T(2,128)(2,1)} %copy-done.21, f32[2,2,320,320]{2,3,1,0:T(8,128)} %get-tuple-element.37, f32[2,2,320]{2,1,0:T(2,128)S(1)} %get-tuple-element.36), kind=kOutput, calls=%fused_computation.60 | convolution fusion | flops 107890240 | bytes 3937280 | tf_op jit(solution)/shard_map/bhqk,bqhd->bkhd/dot_general | solution.py:32
  54.0 2.7 %fusion.98 = bf16[2,320,2,128]{3,1,2,0:T(8,128)(2,1)} fusion(bf16[2,320,2,128]{3,2,1,0:T(2,128)(2,1)} %reshape.152, f32[2,2,320,320]{2,3,1,0:T(8,128)} %get-tuple-element.37, f32[2,2,320]{2,1,0:T(2,128)S(1)} %get-tuple-element.36), kind=kOutput, calls=%fused_computation.66 | convolution fusion | flops 105840640 | bytes 2298880 | tf_op jit(solution)/shard_map/bhqk,bqhd->bkhd/dot_general | solution.py:27
  57.0 2.3 %fusion.241 = (f32[2,2,320]{2,1,0:T(2,128)S(1)}, f32[2,2,320,320]{2,3,1,0:T(8,128)}) fusion(pred[2,320,320]{1,2,0:T(8,128)(4,1)S(1)} %fusion.124, bf16[2,320,2,128]{3,2,1,0:T(2,128)(2,1)S(1)} %reshape.155, bf16[2,320,2,128]{3,2,1,0:T(2,128)(2,1)S(1)} %reshape.154), kind=kOutput, calls=%fused_computation.202 | convolution fusion | flops 106496320 | bytes 2503680 | tf_op jit(solution)/shard_map/sub | solution.py:24
  59.8 3.6 %fusion.90 = bf16[2,320,2,128]{3,1,2,0:T(8,128)(2,1)} fusion(f32[2,2,320,320]{2,3,1,0:T(8,128)S(1)} %fusion.129, bf16[2,320,2,128]{3,2,1,0:T(2,128)(2,1)S(1)} %reshape.154, f32[2,2,320,320]{2,3,1,0:T(8,128)} %get-tuple-element.35, f32[2,2,320]{2,1,0:T(2,128)S(1)} %get-tuple-element.34), kind=kOutput, calls=%fused_computation.62 | convolution fusion | flops 107890240 | bytes 3937280 | tf_op jit(solution)/shard_map/bhqk,bqhd->bkhd/dot_general | solution.py:32
  63.4 3.7 %fusion.93 = bf16[2,320,2,128]{3,1,2,0:T(8,128)(2,1)} fusion(f32[2,2,320,320]{2,3,1,0:T(8,128)S(1)} %fusion.129, bf16[2,320,2,128]{3,2,1,0:T(2,128)(2,1)S(1)} %reshape.155, f32[2,2,320,320]{2,3,1,0:T(8,128)} %get-tuple-element.35, f32[2,2,320]{2,1,0:T(2,128)S(1)} %get-tuple-element.34), kind=kOutput, calls=%fused_computation.63 | convolution fusion | flops 107890240 | bytes 3937280 | tf_op jit(solution)/shard_map/bhqk,bkhd->bqhd/dot_general | solution.py:31
  67.1 2.7 %fusion.99 = bf16[2,320,2,128]{3,1,2,0:T(8,128)(2,1)} fusion(bf16[2,320,2,128]{3,2,1,0:T(2,128)(2,1)S(1)} %reshape.156, f32[2,2,320,320]{2,3,1,0:T(8,128)} %get-tuple-element.35, f32[2,2,320]{2,1,0:T(2,128)S(1)} %get-tuple-element.34), kind=kOutput, calls=%fused_computation.67 | convolution fusion | flops 105840640 | bytes 2298880 | tf_op jit(solution)/shard_map/bhqk,bqhd->bkhd/dot_general | solution.py:27
  75.5 2.0 copy.41
  78.7 2.0 copy.43
  80.7 1.9 stack.58
  86.1 2.0 copy.50
  88.2 1.9 stack.60
  90.1 1.7 constant_dynamic-update-slice_fusion.11
  91.8 2.0 copy.54
  93.8 1.9 stack.62
  96.4 1.7 constant_dynamic-update-slice_fusion.9
  99.6 11.0 %psum.14 = f32[3,4096]{1,0:T(4,128)S(1)} all-reduce(f32[3,4096]{1,0:T(4,128)S(1)} %maximum_dynamic-update-slice_fusion), channel_id=1, replica_groups=mesh['section'=2,'dp'=4,'mp'=4] {'mp'}, use_global_device_ids=true, to_apply=%region_16.17 | all-reduce | flops 12288 | bytes 98304 | tf_op jit(solution)/shard_map/psum | solution.py:87
  110.6 16.8 %psum.15 = f32[3,4096]{1,0:T(4,128)} all-reduce(f32[3,4096]{1,0:T(4,128)S(1)} %psum.14), channel_id=1, replica_groups=mesh['section'=2,'dp'=4,'mp'=4] {'dp'}, use_global_device_ids=true, to_apply=%region_17.18 | all-reduce | flops 12288 | bytes 98304 | tf_op jit(solution)/shard_map/psum | solution.py:88
  129.6 1.4 collective-permute-start
  131.9 1.4 collective-permute-start.1
  134.2 1.4 collective-permute-start.2
  143.0 4.0 %collective-permute-done.2 = bf16[3,160,256]{2,1,0:T(8,128)(2,1)S(1)} collective-permute-done((bf16[3,160,256]{2,1,0:T(8,128)(2,1)}, bf16[3,160,256]{2,1,0:T(8,128)(2,1)S(1)}, u32[]{:S(2)}, u32[]{:S(2)}) %collective-permute-start.2) | collective-permute-done | bytes 245792 | tf_op jit(solution)/shard_map/ppermute | solution.py:82
  148.2 3.9 %collective-permute-done.3 = bf16[3,160,256]{2,1,0:T(8,128)(2,1)S(1)} collective-permute-done((bf16[3,160,256]{2,1,0:T(8,128)(2,1)}, bf16[3,160,256]{2,1,0:T(8,128)(2,1)S(1)}, u32[]{:S(2)}, u32[]{:S(2)}) %collective-permute-start.3) | collective-permute-done | bytes 245792 | tf_op jit(solution)/shard_map/ppermute | solution.py:82
  153.4 11.8 %collective-permute-done.4 = bf16[3,160,256]{2,1,0:T(8,128)(2,1)S(1)} collective-permute-done((bf16[3,160,256]{2,1,0:T(8,128)(2,1)}, bf16[3,160,256]{2,1,0:T(8,128)(2,1)S(1)}, u32[]{:S(2)}, u32[]{:S(2)}) %collective-permute-start.4) | collective-permute-done | bytes 245792 | tf_op jit(solution)/shard_map/ppermute | solution.py:82
  166.5 4.0 %collective-permute-done.5 = bf16[3,160,256]{2,1,0:T(8,128)(2,1)S(1)} collective-permute-done((bf16[3,160,256]{2,1,0:T(8,128)(2,1)}, bf16[3,160,256]{2,1,0:T(8,128)(2,1)S(1)}, u32[]{:S(2)}, u32[]{:S(2)}) %collective-permute-start.5) | collective-permute-done | bytes 245792 | tf_op jit(solution)/shard_map/ppermute | solution.py:82
  172.5 3.0 %collective-permute-done.6 = bf16[3,160,256]{2,1,0:T(8,128)(2,1)S(1)} collective-permute-done((bf16[3,160,256]{2,1,0:T(8,128)(2,1)S(1)}, bf16[3,160,256]{2,1,0:T(8,128)(2,1)S(1)}, u32[]{:S(2)}, u32[]{:S(2)}) %collective-permute-start.6) | collective-permute-done | bytes 245792 | tf_op jit(solution)/shard_map/ppermute | solution.py:82
  178.4 2.3 %collective-permute-done.7 = bf16[3,160,256]{2,1,0:T(8,128)(2,1)S(1)} collective-permute-done((bf16[3,160,256]{2,1,0:T(8,128)(2,1)S(1)}, bf16[3,160,256]{2,1,0:T(8,128)(2,1)S(1)}, u32[]{:S(2)}, u32[]{:S(2)}) %collective-permute-start.7) | collective-permute-done | bytes 245792 | tf_op jit(solution)/shard_map/ppermute | solution.py:82
  184.7 3.8 %collective-permute-done.10 = bf16[3,160,256]{2,1,0:T(8,128)(2,1)S(1)} collective-permute-done((bf16[3,160,256]{2,1,0:T(8,128)(2,1)S(1)}, bf16[3,160,256]{2,1,0:T(8,128)(2,1)S(1)}, u32[]{:S(2)}, u32[]{:S(2)}) %collective-permute-start.10) | collective-permute-done | bytes 245792 | tf_op jit(solution)/shard_map/ppermute | solution.py:82
  189.9 3.9 %collective-permute-done.11 = bf16[3,160,256]{2,1,0:T(8,128)(2,1)S(1)} collective-permute-done((bf16[3,160,256]{2,1,0:T(8,128)(2,1)S(1)}, bf16[3,160,256]{2,1,0:T(8,128)(2,1)S(1)}, u32[]{:S(2)}, u32[]{:S(2)}) %collective-permute-start.11) | collective-permute-done | bytes 245792 | tf_op jit(solution)/shard_map/ppermute | solution.py:82
  193.9 14.3 %collective-permute-done.12 = bf16[3,160,256]{2,1,0:T(8,128)(2,1)S(1)} collective-permute-done((bf16[3,160,256]{2,1,0:T(8,128)(2,1)S(1)}, bf16[3,160,256]{2,1,0:T(8,128)(2,1)S(1)}, u32[]{:S(2)}, u32[]{:S(2)}) %collective-permute-start.12) | collective-permute-done | bytes 245792 | tf_op jit(solution)/shard_map/ppermute | solution.py:82
  208.2 5.3 %collective-permute-done.13 = bf16[3,160,256]{2,1,0:T(8,128)(2,1)S(1)} collective-permute-done((bf16[3,160,256]{2,1,0:T(8,128)(2,1)S(1)}, bf16[3,160,256]{2,1,0:T(8,128)(2,1)S(1)}, u32[]{:S(2)}, u32[]{:S(2)}) %collective-permute-start.13) | collective-permute-done | bytes 245792 | tf_op jit(solution)/shard_map/ppermute | solution.py:82
  213.4 3.2 %collective-permute-done.14 = bf16[3,160,256]{2,1,0:T(8,128)(2,1)S(1)} collective-permute-done((bf16[3,160,256]{2,1,0:T(8,128)(2,1)S(1)}, bf16[3,160,256]{2,1,0:T(8,128)(2,1)S(1)}, u32[]{:S(2)}, u32[]{:S(2)}) %collective-permute-start.14) | collective-permute-done | bytes 245792 | tf_op jit(solution)/shard_map/ppermute | solution.py:82
  216.6 2.6 %collective-permute-done.15 = bf16[3,160,256]{2,1,0:T(8,128)(2,1)S(1)} collective-permute-done((bf16[3,160,256]{2,1,0:T(8,128)(2,1)S(1)}, bf16[3,160,256]{2,1,0:T(8,128)(2,1)S(1)}, u32[]{:S(2)}, u32[]{:S(2)}) %collective-permute-start.15) | collective-permute-done | bytes 245792 | tf_op jit(solution)/shard_map/ppermute | solution.py:82
  219.4 1.9 copy-done.1
  (140 shorter events, 47.3 us)
Async XLA Ops:
  0.6 3.2 %copy-start.10 = (bf16[1,1,640,1024]{3,2,1,0:T(8,128)(2,1)S(1)}, bf16[1,1,640,1024]{3,2,1,0:T(8,128)(2,1)}, u32[]{:S(2)}) copy-start(bf16[1,1,640,1024]{3,2,1,0:T(8,128)(2,1)} %param.6) | copy-start | bytes 3932164
  3.0 2.5 %copy-start.26 = (s32[1,1,640]{2,1,0:T(1,128)S(1)}, s32[1,1,640]{2,1,0:T(1,128)}, u32[]{:S(2)}) copy-start(s32[1,1,640]{2,1,0:T(1,128)} %param.9) | copy-start | bytes 7684
  4.8 3.9 %copy-start.11 = (bf16[1,1,640,1024]{3,2,1,0:T(8,128)(2,1)S(1)}, bf16[1,1,640,1024]{3,2,1,0:T(8,128)(2,1)}, u32[]{:S(2)}) copy-start(bf16[1,1,640,1024]{3,2,1,0:T(8,128)(2,1)} %param.7) | copy-start | bytes 3932164
  22.7 2.8 %copy-start.6 = (bf16[640,256]{1,0:T(8,128)(2,1)S(1)}, bf16[640,256]{1,0:T(8,128)(2,1)}, u32[]{:S(2)}) copy-start(bf16[640,256]{1,0:T(8,128)(2,1)} %get-tuple-element.5) | copy-start | bytes 983044
  22.7 2.9 %copy-start.7 = (bf16[640,256]{1,0:T(8,128)(2,1)S(1)}, bf16[640,256]{1,0:T(8,128)(2,1)}, u32[]{:S(2)}) copy-start(bf16[640,256]{1,0:T(8,128)(2,1)} %get-tuple-element.9) | copy-start | bytes 983044
  22.7 3.0 %copy-start.8 = (bf16[640,256]{1,0:T(8,128)(2,1)S(1)}, bf16[640,256]{1,0:T(8,128)(2,1)}, u32[]{:S(2)}) copy-start(bf16[640,256]{1,0:T(8,128)(2,1)} %get-tuple-element.13) | copy-start | bytes 983044
  25.5 1.0 copy-start.9
  25.5 1.7 copy-start.20
  25.7 1.6 copy-start.22
  38.3 2.8 %copy-start.2 = (bf16[640,256]{1,0:T(8,128)(2,1)S(1)}, bf16[640,256]{1,0:T(8,128)(2,1)}, u32[]{:S(2)}) copy-start(bf16[640,256]{1,0:T(8,128)(2,1)} %get-tuple-element.4) | copy-start | bytes 983044
  38.3 2.9 %copy-start.3 = (bf16[640,256]{1,0:T(8,128)(2,1)S(1)}, bf16[640,256]{1,0:T(8,128)(2,1)}, u32[]{:S(2)}) copy-start(bf16[640,256]{1,0:T(8,128)(2,1)} %get-tuple-element.8) | copy-start | bytes 983044
  38.3 3.0 %copy-start.4 = (bf16[640,256]{1,0:T(8,128)(2,1)S(1)}, bf16[640,256]{1,0:T(8,128)(2,1)}, u32[]{:S(2)}) copy-start(bf16[640,256]{1,0:T(8,128)(2,1)} %get-tuple-element.12) | copy-start | bytes 983044
  41.1 1.0 copy-start.5
  41.2 1.8 copy-start.21
  41.3 1.7 copy-start.23
  67.1 2.7 %copy-start.16 = (bf16[2,320,2,128]{3,1,2,0:T(8,128)(2,1)S(1)}, bf16[2,320,2,128]{3,1,2,0:T(8,128)(2,1)}, u32[]{:S(2)}) copy-start(bf16[2,320,2,128]{3,1,2,0:T(8,128)(2,1)} %fusion.75) | copy-start | bytes 983044
  69.8 1.0 copy-start.13
  69.8 1.5 copy-start.12
  71.4 1.0 copy-start.17
  72.0 1.0 copy-start.15
  72.0 1.5 copy-start.14
  73.9 1.0 copy-start.18
  82.6 1.2 copy-start.19
  127.4 10.2 %collective-permute-start.16 = (f32[3,4096]{1,0:T(4,128)}, f32[3,4096]{1,0:T(4,128)S(1)}, u32[]{:S(2)}, u32[]{:S(2)}) collective-permute-start(f32[3,4096]{1,0:T(4,128)} %psum.15), channel_id=1, source_target_pairs={{16,0},{17,1},{18,2},{19,3},{20,4},{21,5},{22,6},{23,7},{24,8},{25... | collective-permute-start | bytes 147464 | tf_op jit(solution)/shard_map/ppermute | solution.py:89
  129.6 6.0 %copy-start = (bf16[3,640,256]{2,1,0:T(8,128)(2,1)S(1)}, bf16[3,640,256]{2,1,0:T(8,128)(2,1)}, u32[]{:S(2)}) copy-start(bf16[3,640,256]{2,1,0:T(8,128)(2,1)} %constant_dynamic-update-slice_fusion.9) | copy-start | bytes 2949124
  129.6 9.4 %collective-permute-start = (bf16[3,160,256]{2,1,0:T(8,128)(2,1)S(1)}, bf16[3,160,256]{2,1,0:T(8,128)(2,1)}, u32[]{:S(2)}, u32[]{:S(2)}) collective-permute-start(bf16[3,160,256]{2,1,0:T(8,128)(2,1)S(1)} %get-tuple-element.21), channel_id=1, source_target_pairs={{16,0},{17,1},{18,2},{19,3},{20,4},{21,5},{22,6},{23,7},{24,8},{25... | collective-permute-start | bytes 737288 | tf_op jit(solution)/shard_map/ppermute | solution.py:82
  131.9 33.4 %copy-start.24 = (bf16[3,160,256]{2,1,0:T(8,128)(2,1)S(1)}, bf16[3,160,256]{2,1,0:T(8,128)(2,1)}, u32[]{:S(2)}) copy-start(bf16[3,160,256]{2,1,0:T(8,128)(2,1)} %get-tuple-element.23) | copy-start | bytes 737284
  131.9 9.8 %collective-permute-start.1 = (bf16[3,160,256]{2,1,0:T(8,128)(2,1)}, bf16[3,160,256]{2,1,0:T(8,128)(2,1)}, u32[]{:S(2)}, u32[]{:S(2)}) collective-permute-start(bf16[3,160,256]{2,1,0:T(8,128)(2,1)} %get-tuple-element.25), channel_id=1, source_target_pairs={{16,0},{17,1},{18,2},{19,3},{20,4},{21,5},{22,6},{23,7},{24,8},{25... | collective-permute-start | bytes 737288 | tf_op jit(solution)/shard_map/ppermute | solution.py:82
  134.2 7.5 %copy-start.25 = (bf16[3,160,256]{2,1,0:T(8,128)(2,1)S(1)}, bf16[3,160,256]{2,1,0:T(8,128)(2,1)}, u32[]{:S(2)}) copy-start(bf16[3,160,256]{2,1,0:T(8,128)(2,1)} %get-tuple-element.28) | copy-start | bytes 737284
  134.2 12.8 %collective-permute-start.2 = (bf16[3,160,256]{2,1,0:T(8,128)(2,1)}, bf16[3,160,256]{2,1,0:T(8,128)(2,1)S(1)}, u32[]{:S(2)}, u32[]{:S(2)}) collective-permute-start(bf16[3,160,256]{2,1,0:T(8,128)(2,1)} %get-tuple-element.29), channel_id=1, source_target_pairs={{16,0},{17,1},{18,2},{19,3},{20,4},{21,5},{22,6},{23,7},{24,8},{25... | collective-permute-start | bytes 737288 | tf_op jit(solution)/shard_map/ppermute | solution.py:82
  136.4 15.7 %collective-permute-start.3 = (bf16[3,160,256]{2,1,0:T(8,128)(2,1)}, bf16[3,160,256]{2,1,0:T(8,128)(2,1)S(1)}, u32[]{:S(2)}, u32[]{:S(2)}) collective-permute-start(bf16[3,160,256]{2,1,0:T(8,128)(2,1)} %get-tuple-element.33), channel_id=1, source_target_pairs={{16,0},{17,1},{18,2},{19,3},{20,4},{21,5},{22,6},{23,7},{24,8},{25... | collective-permute-start | bytes 737288 | tf_op jit(solution)/shard_map/ppermute | solution.py:82
  137.7 27.6 %collective-permute-start.4 = (bf16[3,160,256]{2,1,0:T(8,128)(2,1)}, bf16[3,160,256]{2,1,0:T(8,128)(2,1)S(1)}, u32[]{:S(2)}, u32[]{:S(2)}) collective-permute-start(bf16[3,160,256]{2,1,0:T(8,128)(2,1)} %get-tuple-element.20), channel_id=1, source_target_pairs={{16,1},{17,2},{18,3},{19,0},{20,5},{21,6},{22,7},{23,4},{24,9},{25... | collective-permute-start | bytes 737288 | tf_op jit(solution)/shard_map/ppermute | solution.py:82
  139.0 31.5 %collective-permute-start.5 = (bf16[3,160,256]{2,1,0:T(8,128)(2,1)}, bf16[3,160,256]{2,1,0:T(8,128)(2,1)S(1)}, u32[]{:S(2)}, u32[]{:S(2)}) collective-permute-start(bf16[3,160,256]{2,1,0:T(8,128)(2,1)} %get-tuple-element.24), channel_id=1, source_target_pairs={{16,1},{17,2},{18,3},{19,0},{20,5},{21,6},{22,7},{23,4},{24,9},{25... | collective-permute-start | bytes 737288 | tf_op jit(solution)/shard_map/ppermute | solution.py:82
  141.7 33.8 %collective-permute-start.6 = (bf16[3,160,256]{2,1,0:T(8,128)(2,1)S(1)}, bf16[3,160,256]{2,1,0:T(8,128)(2,1)S(1)}, u32[]{:S(2)}, u32[]{:S(2)}) collective-permute-start(bf16[3,160,256]{2,1,0:T(8,128)(2,1)S(1)} %copy-done.25), channel_id=1, source_target_pairs={{16,1},{17,2},{18,3},{19,0},{20,5},{21,6},{22,7},{23,4},{24,9},{25... | collective-permute-start | bytes 737288 | tf_op jit(solution)/shard_map/ppermute | solution.py:82
  146.9 33.8 %collective-permute-start.7 = (bf16[3,160,256]{2,1,0:T(8,128)(2,1)S(1)}, bf16[3,160,256]{2,1,0:T(8,128)(2,1)S(1)}, u32[]{:S(2)}, u32[]{:S(2)}) collective-permute-start(bf16[3,160,256]{2,1,0:T(8,128)(2,1)S(1)} %get-tuple-element.32), channel_id=1, source_target_pairs={{16,1},{17,2},{18,3},{19,0},{20,5},{21,6},{22,7},{23,4},{24,9},{25... | collective-permute-start | bytes 737288 | tf_op jit(solution)/shard_map/ppermute | solution.py:82
  152.1 29.9 %collective-permute-start.8 = (bf16[3,160,256]{2,1,0:T(8,128)(2,1)S(1)}, bf16[3,160,256]{2,1,0:T(8,128)(2,1)S(1)}, u32[]{:S(2)}, u32[]{:S(2)}) collective-permute-start(bf16[3,160,256]{2,1,0:T(8,128)(2,1)S(1)} %get-tuple-element.19), channel_id=1, source_target_pairs={{16,2},{17,3},{18,0},{19,1},{20,6},{21,7},{22,4},{23,5},{24,10},{2... | collective-permute-start | bytes 737288 | tf_op jit(solution)/shard_map/ppermute | solution.py:82
  165.2 18.1 %collective-permute-start.9 = (bf16[3,160,256]{2,1,0:T(8,128)(2,1)S(1)}, bf16[3,160,256]{2,1,0:T(8,128)(2,1)S(1)}, u32[]{:S(2)}, u32[]{:S(2)}) collective-permute-start(bf16[3,160,256]{2,1,0:T(8,128)(2,1)S(1)} %copy-done.24), channel_id=1, source_target_pairs={{16,2},{17,3},{18,0},{19,1},{20,6},{21,7},{22,4},{23,5},{24,10},{2... | collective-permute-start | bytes 737288 | tf_op jit(solution)/shard_map/ppermute | solution.py:82
  170.5 18.0 %collective-permute-start.10 = (bf16[3,160,256]{2,1,0:T(8,128)(2,1)S(1)}, bf16[3,160,256]{2,1,0:T(8,128)(2,1)S(1)}, u32[]{:S(2)}, u32[]{:S(2)}) collective-permute-start(bf16[3,160,256]{2,1,0:T(8,128)(2,1)S(1)} %get-tuple-element.27), channel_id=1, source_target_pairs={{16,2},{17,3},{18,0},{19,1},{20,6},{21,7},{22,4},{23,5},{24,10},{2... | collective-permute-start | bytes 737288 | tf_op jit(solution)/shard_map/ppermute | solution.py:82
  175.5 18.3 %collective-permute-start.11 = (bf16[3,160,256]{2,1,0:T(8,128)(2,1)S(1)}, bf16[3,160,256]{2,1,0:T(8,128)(2,1)S(1)}, u32[]{:S(2)}, u32[]{:S(2)}) collective-permute-start(bf16[3,160,256]{2,1,0:T(8,128)(2,1)S(1)} %get-tuple-element.31), channel_id=1, source_target_pairs={{16,2},{17,3},{18,0},{19,1},{20,6},{21,7},{22,4},{23,5},{24,10},{2... | collective-permute-start | bytes 737288 | tf_op jit(solution)/shard_map/ppermute | solution.py:82
  180.8 27.4 %collective-permute-start.12 = (bf16[3,160,256]{2,1,0:T(8,128)(2,1)S(1)}, bf16[3,160,256]{2,1,0:T(8,128)(2,1)S(1)}, u32[]{:S(2)}, u32[]{:S(2)}) collective-permute-start(bf16[3,160,256]{2,1,0:T(8,128)(2,1)S(1)} %get-tuple-element.18), channel_id=1, source_target_pairs={{16,3},{17,0},{18,1},{19,2},{20,7},{21,4},{22,5},{23,6},{24,11},{2... | collective-permute-start | bytes 737288 | tf_op jit(solution)/shard_map/ppermute | solution.py:82
  182.1 31.4 %collective-permute-start.13 = (bf16[3,160,256]{2,1,0:T(8,128)(2,1)S(1)}, bf16[3,160,256]{2,1,0:T(8,128)(2,1)S(1)}, u32[]{:S(2)}, u32[]{:S(2)}) collective-permute-start(bf16[3,160,256]{2,1,0:T(8,128)(2,1)S(1)} %get-tuple-element.22), channel_id=1, source_target_pairs={{16,3},{17,0},{18,1},{19,2},{20,7},{21,4},{22,5},{23,6},{24,11},{2... | collective-permute-start | bytes 737288 | tf_op jit(solution)/shard_map/ppermute | solution.py:82
  183.4 33.2 %collective-permute-start.14 = (bf16[3,160,256]{2,1,0:T(8,128)(2,1)S(1)}, bf16[3,160,256]{2,1,0:T(8,128)(2,1)S(1)}, u32[]{:S(2)}, u32[]{:S(2)}) collective-permute-start(bf16[3,160,256]{2,1,0:T(8,128)(2,1)S(1)} %get-tuple-element.26), channel_id=1, source_target_pairs={{16,3},{17,0},{18,1},{19,2},{20,7},{21,4},{22,5},{23,6},{24,11},{2... | collective-permute-start | bytes 737288 | tf_op jit(solution)/shard_map/ppermute | solution.py:82
  188.5 30.8 %collective-permute-start.15 = (bf16[3,160,256]{2,1,0:T(8,128)(2,1)S(1)}, bf16[3,160,256]{2,1,0:T(8,128)(2,1)S(1)}, u32[]{:S(2)}, u32[]{:S(2)}) collective-permute-start(bf16[3,160,256]{2,1,0:T(8,128)(2,1)S(1)} %get-tuple-element.30), channel_id=1, source_target_pairs={{16,3},{17,0},{18,1},{19,2},{20,7},{21,4},{22,5},{23,6},{24,11},{2... | collective-permute-start | bytes 737288 | tf_op jit(solution)/shard_map/ppermute | solution.py:82
  219.4 1.9 copy-start.1
